TPU v7x, 256 devices: a whole 4x4x8 slice. The times are simulated.
256 devices in a mesh: band: 8 (over y, x_hi), chan: 32 (over x_lo, z, core).
Axes of the slice: x: 4 (x_hi: 2, x_lo: 2; x = x_hi * 2 + x_lo), y: 4, z: 8, core: 2. Of those that a mesh axis runs over, the one named last changes fastest.
Arguments:
- spectra: bfloat16 [2, 64, 512, 8192], P(None, 'band', None, 'chan'), may hold values from -800 to 800
- valid_mask: int32 [512, 8192], P(None, 'chan'), may hold values 0 or 1
Outputs:
- cross_stack: bfloat16 [4, 2, 64, 8192, 256], P(None, None, 'band', 'chan')
All inputs are finite; a program needn't handle non-finite values. No bound on the sum of `valid_mask` on one device may be relied on, other than what follows from the above.
Results may differ from a plain program's by a relative error of at most 0.0053.
Values may be sent and summed in bfloat16 or wider, within the bound.
No kernel may reach another device: no remote copies, remote signals or barrier semaphores. Data moves between devices by JAX's collectives and lax.ppermute only.
A program may use at most 64 MiB of HBM per device.

v0:
```python
import math
import jax
import jax.numpy as jnp
from jax import lax
from jax.sharding import PartitionSpec as P

ROUNDS = 3
eps_energy = 1e-06


def passed_along(value, axis, steps):
    count = lax.axis_size(axis)
    pairs = [(source, (source + steps) % count) for source in range(count)]
    return lax.ppermute(value, axis, pairs)


def cross_block(own_block, partner, scale):
    flipped = jnp.stack([partner[1], -partner[0]])
    real_part = jnp.einsum("pfwa,pfwb->fab", own_block, partner, preferred_element_type=jnp.float32)
    imag_part = jnp.einsum("pfwa,pfwb->fab", own_block, flipped, preferred_element_type=jnp.float32)
    return (jnp.stack([real_part, imag_part]) * scale).astype(jnp.bfloat16)


def shards(spectra, valid_mask):
    values = spectra.astype(jnp.float32)
    partial_energy = jnp.sum(values * values, axis=(0, 1))
    total_bins = spectra.shape[1] * lax.axis_size("band")
    scale = 1.0 / math.sqrt(spectra.shape[2])
    far_count = ROUNDS
    energy = lax.psum(partial_energy, "band")
    window_gain = valid_mask.astype(jnp.float32) / jnp.sqrt(energy / total_bins + eps_energy)
    whitened = (values * window_gain).astype(jnp.bfloat16)
    outputs = [cross_block(whitened, whitened, scale)]
    partners = [whitened]
    carried = whitened
    for round_idx in range(1, far_count + 1):
        carried = passed_along(carried, "chan", 1)
        partners.append(carried)
        outputs.append(cross_block(whitened, carried, scale))
    return jnp.stack(outputs)


def solution(mesh):
    placed = (P(None, "band", None, "chan"), P(None, "chan"))
    return jax.shard_map(
        shards,
        mesh=mesh,
        in_specs=placed,
        out_specs=P(None, None, "band", "chan", None),
        check_vma=False,
    )
```

profile of v0, /device:TPU:2, one launch (start us, length us, event | category | flops | bytes accessed | tf_op | source)
XLA Modules:
  0.0 273.1 jit_solution(12627649000976831893)
XLA Ops:
  6.5 0.0 copy-start
  6.5 0.0 all-reduce.2.cloned.1.call-start
  6.5 3.9 %fusion = f32[512,256]{1,0:T(8,128)} fusion(bf16[2,8,512,256]{3,2,1,0:T(8,128)(2,1)} %param.2), kind=kLoop, calls=%fused_computation.2 | loop fusion | flops 6160384 | bytes 4718592 | tf_op jit(solution)/shard_map/reduce_sum | solution.py:26
  10.4 0.0 all-reduce.2.cloned.1.call-update
  10.5 93.3 %all-reduce.2.cloned.1.call-done = f32[512,256]{1,0:T(8,128)} async-done(((f32[512,256]{1,0:T(8,128)}), f32[512,256]{1,0:T(8,128)}) %all-reduce.2.cloned.1.call-update) | async-done | bytes 524304 | tf_op jit(solution)/shard_map/psum | solution.py:30
  103.8 0.0 copy-done
  103.8 1.1 rsqrt_multiply_fusion
  104.9 3.1 %fusion.1 = bf16[2,8,512,256]{3,2,0,1:T(8,128)(2,1)S(1)} fusion(f32[512,256]{1,0:T(8,128)S(1)} %rsqrt_multiply_fusion, bf16[2,8,512,256]{3,2,1,0:T(8,128)(2,1)} %param.2), kind=kLoop, calls=%fused_computation.3 | loop fusion | flops 6291456 | bytes 8912896 | tf_op jit(solution)/shard_map/convert_element_type | solution.py:32
  108.0 0.1 collective-permute-start
  108.1 50.0 %collective-permute-done = bf16[2,8,512,256]{3,2,0,1:T(8,128)(2,1)S(1)} collective-permute-done((bf16[2,8,512,256]{3,2,0,1:T(8,128)(2,1)S(1)}, bf16[2,8,512,256]{3,2,0,1:T(8,128)(2,1)S(1)}, u32[]{:S(2)}, u32[]{:S(2)}) %collective-permute-start) | collective-permute-done | bytes 4194336 | tf_op jit(solution)/shard_map/ppermute | solution.py:14
  158.1 0.0 collective-permute-start.1
  158.1 0.3 fusion.38
  158.4 49.8 %collective-permute-done.1 = bf16[2,8,512,256]{3,2,0,1:T(8,128)(2,1)S(1)} collective-permute-done((bf16[2,8,512,256]{3,2,0,1:T(8,128)(2,1)S(1)}, bf16[2,8,512,256]{3,2,0,1:T(8,128)(2,1)S(1)}, u32[]{:S(2)}, u32[]{:S(2)}) %collective-permute-start.1) | collective-permute-done | bytes 4194336 | tf_op jit(solution)/shard_map/ppermute | solution.py:14
  208.2 0.0 collective-permute-start.2
  208.2 1.6 fusion.31
  209.8 1.5 convolution_bitcast_fusion.3
  211.3 0.6 fusion.6
  211.8 0.3 fusion.39
  212.1 1.6 fusion.28
  213.7 1.5 convolution_bitcast_fusion.2
  215.2 0.6 fusion.11
  215.8 0.3 fusion.40
  216.1 1.6 fusion.25
  217.7 1.5 convolution_bitcast_fusion.1
  219.1 0.6 fusion.16
  219.7 38.5 %collective-permute-done.2 = bf16[2,8,512,256]{3,2,0,1:T(8,128)(2,1)S(1)} collective-permute-done((bf16[2,8,512,256]{3,2,0,1:T(8,128)(2,1)S(1)}, bf16[2,8,512,256]{3,2,0,1:T(8,128)(2,1)S(1)}, u32[]{:S(2)}, u32[]{:S(2)}) %collective-permute-start.2) | collective-permute-done | bytes 4194336 | tf_op jit(solution)/shard_map/ppermute | solution.py:14
  258.2 0.3 fusion.41
  258.5 1.8 fusion.22
  260.3 1.5 convolution_bitcast_fusion
  261.8 0.6 fusion.21
  262.4 3.9 %pad_maximum_fusion = bf16[4,2,8,256,256]{4,3,2,1,0:T(8,128)(2,1)} fusion(bf16[1,2,8,256,256]{4,3,2,1,0:T(8,128)(2,1)S(1)} %fusion.21, bf16[1,2,8,256,256]{4,3,2,1,0:T(8,128)(2,1)S(1)} %fusion.16, bf16[1,2,8,256,256]{4,3,2,1,0:T(8,128)(2,1)S(1)} %fusion.11, bf16[1,2,8,256,256]{4,3,2,1,0:T(8,128)(2,1)S(1)} %fusion.6), kind=kLoop, calls=%fused_computation.4 | loop fusion | flops 12582912 | bytes 16777216 | tf_op jit(solution)/shard_map/stack | solution.py:40
Async XLA Ops:
  6.5 97.3 %copy-start = (s32[512,256]{1,0:T(8,128)S(1)}, s32[512,256]{1,0:T(8,128)}, u32[]{:S(2)}) copy-start(s32[512,256]{1,0:T(8,128)} %param.3) | copy-start | bytes 1572868
  6.5 97.3 %all-reduce.2.cloned.1.call-start = ((), (), s32[]{:S(2)}) async-start(), calls=%async_computation | async-start | bytes 1048576 | tf_op jit(solution)/shard_map/psum | solution.py:30
  108.0 50.1 %collective-permute-start = (bf16[2,8,512,256]{3,2,0,1:T(8,128)(2,1)S(1)}, bf16[2,8,512,256]{3,2,0,1:T(8,128)(2,1)S(1)}, u32[]{:S(2)}, u32[]{:S(2)}) collective-permute-start(bf16[2,8,512,256]{3,2,0,1:T(8,128)(2,1)S(1)} %fusion.1), channel_id=1, source_target_pairs={{0,1},{1,2},{2,3},{3,4},{4,5},{5,6},{6,7},{7,8},{8,9},{9,10},{10,1... | collective-permute-start | bytes 12582920 | tf_op jit(solution)/shard_map/ppermute | solution.py:14
  158.1 50.0 %collective-permute-start.1 = (bf16[2,8,512,256]{3,2,0,1:T(8,128)(2,1)S(1)}, bf16[2,8,512,256]{3,2,0,1:T(8,128)(2,1)S(1)}, u32[]{:S(2)}, u32[]{:S(2)}) collective-permute-start(bf16[2,8,512,256]{3,2,0,1:T(8,128)(2,1)S(1)} %collective-permute-done), channel_id=1, source_target_pairs={{0,1},{1,2},{2,3},{3,4},{4,5},{5,6},{6,7},{7,8},{8,9},{9,10},{10,1... | collective-permute-start | bytes 12582920 | tf_op jit(solution)/shard_map/ppermute | solution.py:14
  208.2 50.0 %collective-permute-start.2 = (bf16[2,8,512,256]{3,2,0,1:T(8,128)(2,1)S(1)}, bf16[2,8,512,256]{3,2,0,1:T(8,128)(2,1)S(1)}, u32[]{:S(2)}, u32[]{:S(2)}) collective-permute-start(bf16[2,8,512,256]{3,2,0,1:T(8,128)(2,1)S(1)} %collective-permute-done.1), channel_id=1, source_target_pairs={{0,1},{1,2},{2,3},{3,4},{4,5},{5,6},{6,7},{7,8},{8,9},{9,10},{10,1... | collective-permute-start | bytes 12582920 | tf_op jit(solution)/shard_map/ppermute | solution.py:14
Sparse Core Ops, SparseCore 0:
  10.6 93.1 all-reduce.1
where the time goes:
time: 273 us
  waiting for transfers between devices  232 us (85%)
  other arithmetic  15.4 us (6%)
  between operations  13.5 us (5%)
  matrix products  12.5 us (5%)
    ppermute x3, waiting for transfers between devices, passed_along(): return lax.ppermute(value, axis, pairs)  138 us
    psum x1, waiting for transfers between devices, shards(): energy = lax.psum(partial_energy, 'band')  93.3 us
    dot_general x4, matrix products, cross_block(): jnp.einsum('pfwa,pfwb->fab', own_block, flipped, preferred_element_type=j...  6.57 us
    dot_general x4, matrix products, cross_block(): jnp.einsum('pfwa,pfwb->fab', own_block, partner, preferred_element_type=j...  5.93 us
  transfers between devices with their start and end apart: 4, of which 4 were waited for; matrix products, arithmetic and copies ran while one was open for 4% of the time, Pallas kernels for 0%

commit v1 on v0

--- a/solution.py
+++ b/solution.py
@@ -27,7 +27,7 @@
     total_bins = spectra.shape[1] * lax.axis_size("band")
     scale = 1.0 / math.sqrt(spectra.shape[2])
     far_count = ROUNDS
-    energy = lax.psum(partial_energy, "band")
+    energy = jnp.sum(lax.all_gather(partial_energy, "band"), axis=0)
     window_gain = valid_mask.astype(jnp.float32) / jnp.sqrt(energy / total_bins + eps_energy)
     whitened = (values * window_gain).astype(jnp.bfloat16)
     outputs = [cross_block(whitened, whitened, scale)]

time: 273 us -> 260 us (0.952)
  waiting for transfers between devices: 232 us -> 217 us
    psum x1 -> x0, waiting for transfers between devices: 93.3 us -> none  [shards(): energy = lax.psum(partial_energy, 'band')]
    all_gather x0 -> x1, waiting for transfers between devices: none -> 78.6 us  [shards(): energy = jnp.sum(lax.all_gather(partial_energy, 'band'), axis=0)]
  transfers between devices with their start and end apart: 4 -> 4, of which waited for: 4 -> 4; matrix products, arithmetic and copies ran while one was open for 4% -> 5% of each run, Pallas kernels for 0% -> 0%
where the time goes in v1:
time: 260 us
  waiting for transfers between devices  217 us (83%)
  other arithmetic  16.9 us (6%)
  between operations  13.5 us (5%)
  matrix products  12.5 us (5%)
    ppermute x3, waiting for transfers between devices, passed_along(): return lax.ppermute(value, axis, pairs)  138 us
    all_gather x1, waiting for transfers between devices, shards(): energy = jnp.sum(lax.all_gather(partial_energy, 'band'), axis=0)  78.6 us
    dot_general x4, matrix products, cross_block(): jnp.einsum('pfwa,pfwb->fab', own_block, flipped, preferred_element_type=j...  6.57 us
    dot_general x4, matrix products, cross_block(): jnp.einsum('pfwa,pfwb->fab', own_block, partner, preferred_element_type=j...  5.93 us
  transfers between devices with their start and end apart: 4, of which 4 were waited for; matrix products, arithmetic and copies ran while one was open for 5% of the time, Pallas kernels for 0%

profile of v1, /device:TPU:2, one launch (start us, length us, event | category | flops | bytes accessed | tf_op | source)
XLA Modules:
  0.0 259.9 jit_solution(11961514629881533327)
XLA Ops:
  6.5 0.0 copy-start
  6.5 0.0 all-gather.3.cloned.1.call-start
  6.5 3.9 %fusion = f32[512,256]{1,0:T(8,128)} fusion(bf16[2,8,512,256]{3,2,1,0:T(8,128)(2,1)} %param.2), kind=kLoop, calls=%fused_computation.2 | loop fusion | flops 6160384 | bytes 4718592 | tf_op jit(solution)/shard_map/reduce_sum | solution.py:26
  10.4 0.0 all-gather.3.cloned.1.call-update
  10.5 78.6 %all-gather.3.cloned.1.call-done = f32[4096,256]{1,0:T(8,128)} async-done(((f32[512,256]{1,0:T(8,128)}), f32[4096,256]{1,0:T(8,128)}) %all-gather.3.cloned.1.call-update) | async-done | bytes 4194320 | tf_op jit(solution)/shard_map/all_gather | solution.py:30
  89.1 2.5 reduce_sum.19
  91.6 0.0 copy-done
  91.6 0.1 rsqrt_multiply_fusion
  91.7 3.1 %fusion.1 = bf16[2,8,512,256]{3,2,0,1:T(8,128)(2,1)S(1)} fusion(f32[512,256]{1,0:T(8,128)S(1)} %rsqrt_multiply_fusion, bf16[2,8,512,256]{3,2,1,0:T(8,128)(2,1)} %param.2), kind=kLoop, calls=%fused_computation.3 | loop fusion | flops 6291456 | bytes 8912896 | tf_op jit(solution)/shard_map/convert_element_type | solution.py:32
  94.8 0.1 collective-permute-start
  94.9 50.0 %collective-permute-done = bf16[2,8,512,256]{3,2,0,1:T(8,128)(2,1)S(1)} collective-permute-done((bf16[2,8,512,256]{3,2,0,1:T(8,128)(2,1)S(1)}, bf16[2,8,512,256]{3,2,0,1:T(8,128)(2,1)S(1)}, u32[]{:S(2)}, u32[]{:S(2)}) %collective-permute-start) | collective-permute-done | bytes 4194336 | tf_op jit(solution)/shard_map/ppermute | solution.py:14
  144.9 0.0 collective-permute-start.1
  144.9 0.3 fusion.38
  145.2 49.8 %collective-permute-done.1 = bf16[2,8,512,256]{3,2,0,1:T(8,128)(2,1)S(1)} collective-permute-done((bf16[2,8,512,256]{3,2,0,1:T(8,128)(2,1)S(1)}, bf16[2,8,512,256]{3,2,0,1:T(8,128)(2,1)S(1)}, u32[]{:S(2)}, u32[]{:S(2)}) %collective-permute-start.1) | collective-permute-done | bytes 4194336 | tf_op jit(solution)/shard_map/ppermute | solution.py:14
  195.0 0.0 collective-permute-start.2
  195.0 1.6 fusion.31
  196.6 1.5 convolution_bitcast_fusion.3
  198.0 0.6 fusion.6
  198.6 0.3 fusion.39
  198.9 1.6 fusion.28
  200.5 1.5 convolution_bitcast_fusion.2
  202.0 0.6 fusion.11
  202.6 0.3 fusion.40
  202.9 1.6 fusion.25
  204.5 1.5 convolution_bitcast_fusion.1
  205.9 0.6 fusion.16
  206.5 38.5 %collective-permute-done.2 = bf16[2,8,512,256]{3,2,0,1:T(8,128)(2,1)S(1)} collective-permute-done((bf16[2,8,512,256]{3,2,0,1:T(8,128)(2,1)S(1)}, bf16[2,8,512,256]{3,2,0,1:T(8,128)(2,1)S(1)}, u32[]{:S(2)}, u32[]{:S(2)}) %collective-permute-start.2) | collective-permute-done | bytes 4194336 | tf_op jit(solution)/shard_map/ppermute | solution.py:14
  245.0 0.3 fusion.41
  245.3 1.8 fusion.22
  247.1 1.5 convolution_bitcast_fusion
  248.6 0.6 fusion.21
  249.2 3.9 %pad_maximum_fusion = bf16[4,2,8,256,256]{4,3,2,1,0:T(8,128)(2,1)} fusion(bf16[1,2,8,256,256]{4,3,2,1,0:T(8,128)(2,1)S(1)} %fusion.21, bf16[1,2,8,256,256]{4,3,2,1,0:T(8,128)(2,1)S(1)} %fusion.16, bf16[1,2,8,256,256]{4,3,2,1,0:T(8,128)(2,1)S(1)} %fusion.11, bf16[1,2,8,256,256]{4,3,2,1,0:T(8,128)(2,1)S(1)} %fusion.6), kind=kLoop, calls=%fused_computation.4 | loop fusion | flops 12582912 | bytes 16777216 | tf_op jit(solution)/shard_map/stack | solution.py:40
Async XLA Ops:
  6.5 85.1 %copy-start = (s32[512,256]{1,0:T(8,128)S(1)}, s32[512,256]{1,0:T(8,128)}, u32[]{:S(2)}) copy-start(s32[512,256]{1,0:T(8,128)} %param.3) | copy-start | bytes 1572868
  6.5 82.6 %all-gather.3.cloned.1.call-start = ((), (), s32[]{:S(2)}) async-start(), calls=%async_computation | async-start | bytes 4718592 | tf_op jit(solution)/shard_map/all_gather | solution.py:30
  94.8 50.1 %collective-permute-start = (bf16[2,8,512,256]{3,2,0,1:T(8,128)(2,1)S(1)}, bf16[2,8,512,256]{3,2,0,1:T(8,128)(2,1)S(1)}, u32[]{:S(2)}, u32[]{:S(2)}) collective-permute-start(bf16[2,8,512,256]{3,2,0,1:T(8,128)(2,1)S(1)} %fusion.1), channel_id=1, source_target_pairs={{0,1},{1,2},{2,3},{3,4},{4,5},{5,6},{6,7},{7,8},{8,9},{9,10},{10,1... | collective-permute-start | bytes 12582920 | tf_op jit(solution)/shard_map/ppermute | solution.py:14
  144.9 50.0 %collective-permute-start.1 = (bf16[2,8,512,256]{3,2,0,1:T(8,128)(2,1)S(1)}, bf16[2,8,512,256]{3,2,0,1:T(8,128)(2,1)S(1)}, u32[]{:S(2)}, u32[]{:S(2)}) collective-permute-start(bf16[2,8,512,256]{3,2,0,1:T(8,128)(2,1)S(1)} %collective-permute-done), channel_id=1, source_target_pairs={{0,1},{1,2},{2,3},{3,4},{4,5},{5,6},{6,7},{7,8},{8,9},{9,10},{10,1... | collective-permute-start | bytes 12582920 | tf_op jit(solution)/shard_map/ppermute | solution.py:14
  195.0 50.0 %collective-permute-start.2 = (bf16[2,8,512,256]{3,2,0,1:T(8,128)(2,1)S(1)}, bf16[2,8,512,256]{3,2,0,1:T(8,128)(2,1)S(1)}, u32[]{:S(2)}, u32[]{:S(2)}) collective-permute-start(bf16[2,8,512,256]{3,2,0,1:T(8,128)(2,1)S(1)} %collective-permute-done.1), channel_id=1, source_target_pairs={{0,1},{1,2},{2,3},{3,4},{4,5},{5,6},{6,7},{7,8},{8,9},{9,10},{10,1... | collective-permute-start | bytes 12582920 | tf_op jit(solution)/shard_map/ppermute | solution.py:14
Sparse Core Ops, SparseCore 0:
  10.6 78.4 all-gather.2
